TPU v7x, 32 devices: a whole 2x2x4 slice. The times are simulated.
32 devices in a mesh: lat: 8 (over y, x, core), lon: 4 (over z).
Axes of the slice: x: 2, y: 2, z: 4, core: 2. Of those that a mesh axis runs over, the one named last changes fastest.
Arguments:
- features: bfloat16 [192, 180, 256], P('lat', 'lon'), may hold values from -6 to 6
- obs_mask: int32 [192, 180, 8], P('lat', 'lon'), may hold values 0 or 1
- filter_taps: bfloat16 [192, 4, 3, 17], replicated, may hold values from 0.049804688 to 1
- band_width: int32 [192], replicated, may hold values from 1 to 8, as said below
- mixing: bfloat16 [8, 4, 32, 32], replicated, may hold values from -0.5 to 0.5
- cotangent: bfloat16 [192, 180, 256], P('lat', 'lon'), may hold values from -6 to 6
Outputs:
- infilled: bfloat16 [192, 180, 256], P('lat', 'lon')
- input_grad: bfloat16 [192, 180, 256], P('lat', 'lon')
- weight_grad: float32 [8, 4, 32, 32], replicated
Inputs may be any that keep to these rules, and one draw needn't show every extreme that they name: band_width is 8 at the first and last cycle and 1 at cycle 192 // 2.
All inputs are finite; a program needn't handle non-finite values. No bound on the sum of `obs_mask` on one device may be relied on, other than what follows from the above.
Results may differ from a plain program's by a relative error of at most 0.005.
Values may be sent and summed in bfloat16 or wider, within the bound.
No kernel may reach another device: no remote copies, remote signals or barrier semaphores. Data moves between devices by JAX's collectives and lax.ppermute only.
A program may use at most 128 MiB of HBM per device.

v0:
```python
import math
import jax
import jax.numpy as jnp
from jax import lax
from jax.sharding import PartitionSpec as P


def with_halo(block, sides, width, periodic):
    for axis, dim in sides:
        count = lax.axis_size(axis)
        forward = [(i, i + 1) for i in range(count - 1)]
        if periodic:
            forward.append((count - 1, 0))
        backward = [(target, source) for source, target in forward]
        low = lax.ppermute(
            lax.slice_in_dim(block, block.shape[dim] - width, None, axis=dim), axis, forward
        )
        high = lax.ppermute(lax.slice_in_dim(block, 0, width, axis=dim), axis, backward)
        block = jnp.concatenate([low, block, high], axis=dim)
    return block


def passed_along(block, axis, distance):
    devices = range(lax.axis_size(axis))
    route = [(i - distance, i) for i in devices if i - distance in devices]
    return lax.ppermute(block, axis, route)


def from_behind(x, axis, by):
    size = lax.axis_size(axis)
    return lax.ppermute(x, axis, [(i, (i + by) % size) for i in range(size)])


def local(features, obs_mask, filter_taps, band_width, mixing, cotangent):
    row_count, col_count, chan_count = features.shape
    group_count = obs_mask.shape[2]
    group_width = chan_count // group_count
    basis_count = mixing.shape[1]
    tap_count = filter_taps.shape[3]
    tap_reach = (tap_count - 1) // 2
    padded_cols = col_count + 2 * tap_reach
    mask_values = obs_mask.astype(jnp.bfloat16)
    masked = (
        features.reshape(row_count, col_count, group_count, group_width) * mask_values[..., None]
    ).reshape(row_count, col_count, chan_count)
    wide_input, wide_mask = (
        with_halo(masked, (("lon", 1),), tap_reach, True),
        with_halo(mask_values, (("lon", 1),), tap_reach, True),
    )
    full_input, full_mask = (
        with_halo(wide_input, (("lat", 0),), 1, False),
        with_halo(wide_mask, (("lat", 0),), 1, False),
    )
    offsets = jnp.arange(tap_count) - tap_reach
    allowed = jnp.abs(offsets)[None, :] <= band_width[:, None]
    global_taps = filter_taps * allowed[:, None, None, :].astype(jnp.bfloat16)
    first_row = lax.axis_index("lat") * row_count
    local_taps = lax.dynamic_slice_in_dim(global_taps, first_row, row_count, 0)
    padded_index = jnp.arange(padded_cols)
    output_index = jnp.arange(col_count)
    tap_index = jnp.arange(tap_count)
    forward_table = (
        padded_index[None, :, None] - output_index[None, None, :] == tap_index[:, None, None]
    ).astype(jnp.bfloat16)
    band_blocks = jnp.einsum(
        "ibed,dpj->ibepj", local_taps, forward_table, preferred_element_type=jnp.float32
    ).astype(jnp.bfloat16)
    numerator = jnp.zeros((row_count, basis_count, col_count, chan_count), jnp.float32)
    denominator = jnp.zeros((row_count, basis_count, col_count, group_count), jnp.float32)
    for lat_step in range(3):
        band_block = band_blocks[:, :, lat_step]
        numerator = numerator + jnp.einsum(
            "ibpj,ipc->ibjc",
            band_block,
            full_input[lat_step : lat_step + row_count],
            preferred_element_type=jnp.float32,
        )
        denominator = denominator + jnp.einsum(
            "ibpj,ipg->ibjg",
            band_block,
            full_mask[lat_step : lat_step + row_count],
            preferred_element_type=jnp.float32,
        )
    safe_denom = jnp.maximum(denominator, 1.0)
    scaled = (
        numerator.reshape(row_count, basis_count, col_count, group_count, group_width)
        / safe_denom[..., None]
    ).astype(jnp.bfloat16)
    infilled = (
        jnp.einsum("ibjgc,gbco->ijgo", scaled, mixing, preferred_element_type=jnp.float32)
        .reshape(row_count, col_count, chan_count)
        .astype(jnp.bfloat16)
    )
    upstream = cotangent.reshape(row_count, col_count, group_count, group_width)
    local_grad = jnp.einsum(
        "ibjgc,ijgo->gbco", scaled, upstream, preferred_element_type=jnp.float32
    )
    cell_count = row_count * lax.axis_size("lat") * col_count * lax.axis_size("lon")
    weight_grad = lax.psum(local_grad, ("lat", "lon")) * (1.0 / math.sqrt(cell_count))
    back_prop = jnp.einsum("ijgo,gbco->ibjgc", upstream, mixing, preferred_element_type=jnp.float32)
    pulled = (
        (back_prop / safe_denom[..., None])
        .astype(jnp.bfloat16)
        .reshape(row_count, basis_count, col_count, chan_count)
    )
    collected = jnp.zeros((row_count + 2, padded_cols, chan_count), jnp.float32)
    for lat_step in range(3):
        term_rows = jnp.einsum(
            "ibpj,ibjc->ipc",
            band_blocks[:, :, lat_step],
            pulled,
            preferred_element_type=jnp.float32,
        )
        collected = collected.at[lat_step : lat_step + row_count].add(term_rows)
    from_below = passed_along(collected[0:1], "lat", -1)
    from_above = passed_along(collected[row_count + 1 : row_count + 2], "lat", 1)
    inner_rows = collected[1 : row_count + 1]
    inner_rows = inner_rows.at[row_count - 1 : row_count].add(from_below)
    inner_rows = inner_rows.at[0:1].add(from_above)
    left_rim = inner_rows[:, :tap_reach]
    right_rim = inner_rows[:, col_count + tap_reach :]
    from_right = from_behind(left_rim.astype(jnp.bfloat16), "lon", -1).astype(left_rim.dtype)
    from_left = from_behind(right_rim, "lon", 1)
    gathered = inner_rows[:, tap_reach : tap_reach + col_count]
    gathered = gathered.at[:, col_count - tap_reach :].add(from_right)
    gathered = gathered.at[:, :tap_reach].add(from_left)
    input_grad = (
        (gathered.reshape(row_count, col_count, group_count, group_width) * mask_values[..., None])
        .reshape(row_count, col_count, chan_count)
        .astype(jnp.bfloat16)
    )
    return (infilled, input_grad, weight_grad)


def solution(mesh):
    placed = (P("lat", "lon", None), P("lat", "lon", None), P(), P(), P(), P("lat", "lon", None))
    return jax.shard_map(
        local,
        mesh=mesh,
        in_specs=placed,
        out_specs=(P("lat", "lon", None), P("lat", "lon", None), P()),
        check_vma=False,
    )
```

profile of v0, /device:TPU:0, one launch (start us, length us, event | category | flops | bytes accessed | tf_op | source)
XLA Modules:
  0.0 297.3 jit_solution(17708958694991090387)
XLA Ops:
  7.2 0.9 convert_element_type.43
  8.2 0.1 fusion.56
  8.2 3.1 %collective-permute-start.4 = (bf16[24,8,8]{1,2,0:T(8,128)(2,1)S(1)}, bf16[24,8,8]{1,2,0:T(8,128)(2,1)S(1)}, u32[]{:S(2)}, u32[]{:S(2)}) collective-permute-start(bf16[24,8,8]{1,2,0:T(8,128)(2,1)S(1)} %get-tuple-element.109), channel_id=1, source_target_pairs={{0,1},{1,2},{2,3},{3,0},{4,5},{5,6},{6,7},{7,4},{8,9},{9,10},{10,1... | collective-permute-start | bytes 9224 | tf_op jit(solution)/shard_map/ppermute | solution.py:15
  11.3 2.1 collective-permute-start.5
  13.5 0.3 copy.59
  13.7 0.8 compare_convert_fusion
  14.5 0.1 copy.57
  14.6 1.0 constant_dynamic-slice_fusion
  15.6 0.2 copy.113
  15.8 1.4 mul.42
  17.2 2.3 mul.43
  19.5 1.0 convolution_convert_fusion
  20.5 1.6 slice_bitcast_fusion
  22.1 0.2 copy_multiply_fusion.1
  22.3 3.9 %reshape.274 = bf16[24,45,8,32]{3,2,0,1:T(8,128)(2,1)} reshape(bf16[24,45,256]{2,0,1:T(8,128)(2,1)} %param.25) | data formatting | bytes 1105920 | tf_op jit(solution)/shard_map/reshape | solution.py:94
  26.2 4.9 %copy.97 = bf16[24,45,8,32,1]{1,3,0,4,2:T(8,128)(2,1)} copy(bf16[24,45,8,32,1]{3,2,0,1,4:T(8,128)(2,1)} %bitcast.110) | data formatting | bytes 1105920 | tf_op jit(solution)/shard_map/reshape | solution.py:94
  31.2 0.1 pad_maximum_fusion.21
  31.3 1.6 collective-permute-start.6
  32.9 1.5 collective-permute-start.7
  34.4 1.2 fusion.14
  35.6 2.1 collective-permute-done.7
  37.7 1.2 fusion.7
  38.9 1.2 fusion.4
  40.1 0.2 copy.69
  40.4 3.7 %fusion = bf16[24,4,45,8,32]{2,4,0,1,3:T(8,128)(2,1)} fusion(f32[24,4,45,8]{2,0,1,3:T(8,128)S(1)} %copy.69, bf16[24,45,8,32,1]{1,3,0,4,2:T(8,128)(2,1)S(1)} %copy-done.15, bf16[8,4,32,32]{3,2,1,0:T(8,128)(2,1)S(1)} %copy-done), kind=kOutput, calls=%fused_computation.1 | convolution fusion | flops 72990720 | bytes 2968576 | tf_op jit(solution)/shard_map/ijgo,gbco->ibjgc/dot_general | solution.py:100
  44.1 12.5 %copy.111 = bf16[24,4,45,8,32]{4,3,2,1,0:T(8,128)(2,1)} copy(bf16[24,4,45,8,32]{2,4,0,1,3:T(8,128)(2,1)} %fusion) | data formatting | bytes 4423680 | tf_op jit(solution)/shard_map/reshape | solution.py:104
  56.6 10.6 %reshape.294 = bf16[24,4,45,256]{3,2,1,0:T(8,128)(2,1)S(1)} reshape(bf16[24,4,45,8,32]{4,3,2,1,0:T(8,128)(2,1)} %copy.111) | data formatting | bytes 4423680 | tf_op jit(solution)/shard_map/reshape | solution.py:104
  67.2 1.9 convolution_bitcast_fusion
  69.1 0.2 scatter-add.24
  69.2 1.1 copy-done.6
  70.3 0.8 fusion.1
  71.1 0.4 copy-done.9
  71.5 2.1 constant_dynamic-update-slice_fusion
  73.6 1.2 copy-done.1
  74.9 1.3 collective-permute-start.8
  76.3 3.8 %collective-permute-start.1 = (bf16[24,8,256]{2,1,0:T(8,128)(2,1)S(1)}, bf16[24,8,256]{2,1,0:T(8,128)(2,1)S(1)}, u32[]{:S(2)}, u32[]{:S(2)}) collective-permute-start(bf16[24,8,256]{2,1,0:T(8,128)(2,1)S(1)} %get-tuple-element.106), channel_id=1, source_target_pairs={{1,0},{2,1},{3,2},{0,3},{5,4},{6,5},{7,6},{4,7},{9,8},{10,9},{11,1... | collective-permute-start | bytes 294920 | tf_op jit(solution)/shard_map/ppermute | solution.py:18
  80.1 0.3 copy.82
  80.3 3.2 %mul.45 = f32[24,45,8,32]{3,2,0,1:T(8,128)} broadcast(f32[24,45,8]{2,0,1:T(8,128)S(1)} %copy.82), dimensions={0,1,2} | broadcast | bytes 1140480 | tf_op jit(solution)/shard_map/mul | solution.py:128
  83.5 4.5 %mul.46 = f32[24,45,256]{2,0,1:T(8,128)} reshape(f32[24,45,8,32]{3,2,0,1:T(8,128)} %mul.45) | data formatting | bytes 2211840 | tf_op jit(solution)/shard_map/mul | solution.py:128
  88.0 0.1 slice.279
  88.2 1.0 fusion.52
  89.1 4.3 %collective-permute-start.9 = (f32[1,61,256]{2,1,0:T(8,128)S(1)}, f32[1,61,256]{2,1,0:T(8,128)S(1)}, u32[]{:S(2)}, u32[]{:S(2)}) collective-permute-start(f32[1,61,256]{2,1,0:T(8,128)S(1)} %get-tuple-element.101), channel_id=1, source_target_pairs={{0,4},{4,8},{8,12},{12,16},{16,20},{20,24},{24,28},{1,5},{5,9},{9,... | collective-permute-start | bytes 187400 | tf_op jit(solution)/shard_map/ppermute | solution.py:26
  93.5 0.1 pad_maximum_fusion.10
  93.6 1.3 collective-permute-start.3
  94.9 4.8 %collective-permute-start.2 = (bf16[1,61,256]{2,1,0:T(8,128)(2,1)S(1)}, bf16[1,61,256]{2,1,0:T(8,128)(2,1)S(1)}, u32[]{:S(2)}, u32[]{:S(2)}) collective-permute-start(bf16[1,61,256]{2,1,0:T(8,128)(2,1)S(1)} %get-tuple-element.104), channel_id=1, source_target_pairs={{0,4},{4,8},{8,12},{12,16},{16,20},{20,24},{24,28},{1,5},{5,9},{9,... | collective-permute-start | bytes 93704 | tf_op jit(solution)/shard_map/ppermute | solution.py:15
  99.8 0.8 fusion.16
  100.6 1.1 slice.284
  101.7 0.7 copy-done.4
  102.5 0.8 fusion.20
  103.2 3.0 add_add_fusion
  106.2 11.7 %reshape.293 = f32[24,4,45,8,32]{4,3,2,1,0:T(8,128)} reshape(f32[24,4,45,256]{3,2,1,0:T(8,128)} %add_add_fusion) | data formatting | bytes 8847360 | tf_op jit(solution)/shard_map/reshape | solution.py:86
  117.9 17.1 %copy.70 = f32[24,4,45,8,32]{2,4,0,1,3:T(8,128)} copy(f32[24,4,45,8,32]{4,3,2,1,0:T(8,128)} %reshape.293) | data formatting | bytes 8847360 | tf_op jit(solution)/shard_map/reshape | solution.py:86
  135.0 9.5 %divide_convert_fusion = bf16[24,4,45,8,32]{2,4,0,1,3:T(8,128)(2,1)} fusion(f32[24,4,45,8,32]{2,4,0,1,3:T(8,128)} %copy.70, f32[24,4,45,8]{2,0,1,3:T(8,128)S(1)} %copy-done.18), kind=kLoop, calls=%fused_computation.2 | loop fusion | flops 2211840 | bytes 6773760 | tf_op jit(solution)/shard_map/convert_element_type | solution.py:88
  144.5 5.4 %convolution_bitcast_fusion.1 = f32[8,4,32,32]{3,2,1,0:T(8,128)} fusion(bf16[24,4,45,8,32]{2,4,0,1,3:T(8,128)(2,1)} %divide_convert_fusion, bf16[24,45,8,32,1]{1,3,0,4,2:T(8,128)(2,1)S(1)} %copy-done.16), kind=kOutput, calls=%fused_computation.11 | convolution fusion | flops 70778880 | bytes 2895872 | tf_op jit(solution)/shard_map/ibjgc,ijgo->gbco/dot_general | solution.py:95
  149.8 4.9 %fusion.2 = bf16[24,45,8,32]{1,3,0,2:T(8,128)(2,1)} fusion(bf16[24,4,45,8,32]{2,4,0,1,3:T(8,128)(2,1)} %divide_convert_fusion, bf16[8,4,32,32]{3,2,1,0:T(8,128)(2,1)S(1)} %copy-done), kind=kOutput, calls=%fused_computation.9 | convolution fusion | flops 71055360 | bytes 2830336 | tf_op jit(solution)/shard_map/ibjgc,gbco->ijgo/dot_general | solution.py:90
  154.8 5.2 %copy.73 = bf16[24,45,8,32]{3,2,0,1:T(8,128)(2,1)S(1)} copy(bf16[24,45,8,32]{1,3,0,2:T(8,128)(2,1)} %fusion.2) | data formatting | bytes 1105920 | tf_op jit(solution)/shard_map/convert_element_type | solution.py:92
  160.0 2.3 convert_element_type.47
  162.4 1.3 fusion.51
  163.7 1.4 collective-permute-start.11
  165.1 121.7 %all-reduce.3.cloned.1.call-done = f32[8,4,32,32]{3,2,1,0:T(8,128)} async-done(((f32[8,4,32,32]{3,2,1,0:T(8,128)}), f32[8,4,32,32]{3,2,1,0:T(8,128)}) %all-reduce.3.cloned.1.call-update) | async-done | bytes 131088 | tf_op jit(solution)/shard_map/psum | solution.py:99
  286.7 1.9 broadcast_multiply_fusion
  288.6 0.3 scatter-add.31
  289.0 0.5 fusion.5
  289.4 1.0 copy.85
  (61 shorter events, 0.4 us)
Async XLA Ops:
  7.2 33.2 %copy-start = (bf16[8,4,32,32]{3,2,1,0:T(8,128)(2,1)S(1)}, bf16[8,4,32,32]{3,2,1,0:T(8,128)(2,1)}, u32[]{:S(2)}) copy-start(bf16[8,4,32,32]{3,2,1,0:T(8,128)(2,1)} %param.24) | copy-start | bytes 196612
  7.2 279.5 %all-reduce.3.cloned.1.call-start = ((), (), s32[]{:S(2)}) async-start(), calls=%async_computation | async-start | bytes 1048576 | tf_op jit(solution)/shard_map/psum | solution.py:99
  8.2 22.9 %collective-permute-start.4 = (bf16[24,8,8]{1,2,0:T(8,128)(2,1)S(1)}, bf16[24,8,8]{1,2,0:T(8,128)(2,1)S(1)}, u32[]{:S(2)}, u32[]{:S(2)}) collective-permute-start(bf16[24,8,8]{1,2,0:T(8,128)(2,1)S(1)} %get-tuple-element.109), channel_id=1, source_target_pairs={{0,1},{1,2},{2,3},{3,0},{4,5},{5,6},{6,7},{7,4},{8,9},{9,10},{10,1... | collective-permute-start | bytes 9224 | tf_op jit(solution)/shard_map/ppermute | solution.py:15
  11.3 19.8 %collective-permute-start.5 = (bf16[24,8,8]{1,2,0:T(8,128)(2,1)S(1)}, bf16[24,8,8]{1,2,0:T(8,128)(2,1)S(1)}, u32[]{:S(2)}, u32[]{:S(2)}) collective-permute-start(bf16[24,8,8]{1,2,0:T(8,128)(2,1)S(1)} %get-tuple-element.110), channel_id=1, source_target_pairs={{1,0},{2,1},{3,2},{0,3},{5,4},{6,5},{7,6},{4,7},{9,8},{10,9},{11,1... | collective-permute-start | bytes 9224 | tf_op jit(solution)/shard_map/ppermute | solution.py:18
  20.5 1.6 copy-start.14
  20.5 1.6 copy-start.19
  22.1 12.2 %copy-start.5 = (bf16[24,4,61,45]{2,0,3,1:T(8,128)(2,1)}, bf16[24,4,61,45]{2,0,3,1:T(8,128)(2,1)S(1)}, u32[]{:S(2)}) copy-start(bf16[24,4,61,45]{2,0,3,1:T(8,128)(2,1)S(1)} %get-tuple-element.97) | copy-start | bytes 1581124
  22.1 16.8 %copy-start.3 = (bf16[24,4,61,45]{2,0,3,1:T(8,128)(2,1)}, bf16[24,4,61,45]{2,0,3,1:T(8,128)(2,1)S(1)}, u32[]{:S(2)}) copy-start(bf16[24,4,61,45]{2,0,3,1:T(8,128)(2,1)S(1)} %get-tuple-element.98) | copy-start | bytes 1581124
  31.2 6.5 %copy-start.8 = (bf16[24,4,61,45]{2,0,3,1:T(8,128)(2,1)S(1)}, bf16[24,4,61,45]{2,0,3,1:T(8,128)(2,1)}, u32[]{:S(2)}) copy-start(bf16[24,4,61,45]{2,0,3,1:T(8,128)(2,1)} %get-tuple-element.96) | copy-start | bytes 1581124
  31.3 7.6 %collective-permute-start.6 = (bf16[1,61,8]{1,2,0:T(8,128)(2,1)S(1)}, bf16[1,61,8]{1,2,0:T(8,128)(2,1)S(1)}, u32[]{:S(2)}, u32[]{:S(2)}) collective-permute-start(bf16[1,61,8]{1,2,0:T(8,128)(2,1)S(1)} %get-tuple-element.107), channel_id=1, source_target_pairs={{0,4},{4,8},{8,12},{12,16},{16,20},{20,24},{24,28},{1,5},{5,9},{9,... | collective-permute-start | bytes 2936 | tf_op jit(solution)/shard_map/ppermute | solution.py:15
  32.9 4.8 %collective-permute-start.7 = (bf16[1,61,8]{1,2,0:T(8,128)(2,1)S(1)}, bf16[1,61,8]{1,2,0:T(8,128)(2,1)S(1)}, u32[]{:S(2)}, u32[]{:S(2)}) collective-permute-start(bf16[1,61,8]{1,2,0:T(8,128)(2,1)S(1)} %get-tuple-element.108), channel_id=1, source_target_pairs={{4,0},{8,4},{12,8},{16,12},{20,16},{24,20},{28,24},{5,1},{9,5},{13... | collective-permute-start | bytes 2936 | tf_op jit(solution)/shard_map/ppermute | solution.py:18
  38.9 1.5 copy-start.15
  40.4 3.7 %copy-start.17 = (f32[24,4,45,8]{2,0,1,3:T(8,128)}, f32[24,4,45,8]{2,0,1,3:T(8,128)S(1)}, u32[]{:S(2)}) copy-start(f32[24,4,45,8]{2,0,1,3:T(8,128)S(1)} %copy.69) | copy-start | bytes 414724
  69.1 1.2 copy-start.6
  70.3 1.2 copy-start.9
  73.6 1.2 copy-start.1
  74.9 13.3 %collective-permute-start.8 = (f32[1,61,256]{2,1,0:T(8,128)S(1)}, f32[1,61,256]{2,1,0:T(8,128)S(1)}, u32[]{:S(2)}, u32[]{:S(2)}) collective-permute-start(f32[1,61,256]{2,1,0:T(8,128)S(1)} %slice.281), channel_id=1, source_target_pairs={{4,0},{8,4},{12,8},{16,12},{20,16},{24,20},{28,24},{5,1},{9,5},{13... | collective-permute-start | bytes 187400 | tf_op jit(solution)/shard_map/ppermute | solution.py:26
  76.2 17.3 %collective-permute-start = (bf16[24,8,256]{2,1,0:T(8,128)(2,1)S(1)}, bf16[24,8,256]{2,1,0:T(8,128)(2,1)S(1)}, u32[]{:S(2)}, u32[]{:S(2)}) collective-permute-start(bf16[24,8,256]{2,1,0:T(8,128)(2,1)S(1)} %get-tuple-element.105), channel_id=1, source_target_pairs={{0,1},{1,2},{2,3},{3,0},{4,5},{5,6},{6,7},{7,4},{8,9},{9,10},{10,1... | collective-permute-start | bytes 294920 | tf_op jit(solution)/shard_map/ppermute | solution.py:15
  76.3 17.2 %collective-permute-start.1 = (bf16[24,8,256]{2,1,0:T(8,128)(2,1)S(1)}, bf16[24,8,256]{2,1,0:T(8,128)(2,1)S(1)}, u32[]{:S(2)}, u32[]{:S(2)}) collective-permute-start(bf16[24,8,256]{2,1,0:T(8,128)(2,1)S(1)} %get-tuple-element.106), channel_id=1, source_target_pairs={{1,0},{2,1},{3,2},{0,3},{5,4},{6,5},{7,6},{4,7},{9,8},{10,9},{11,1... | collective-permute-start | bytes 294920 | tf_op jit(solution)/shard_map/ppermute | solution.py:18
  83.5 4.5 %copy-start.2 = (f32[26,61,256]{2,1,0:T(8,128)S(1)}, f32[26,61,256]{2,1,0:T(8,128)}, u32[]{:S(2)}) copy-start(f32[26,61,256]{2,1,0:T(8,128)} %copy-done.1) | copy-start | bytes 4872196
  88.1 11.6 %copy-start.7 = (bf16[24,4,61,45]{2,0,3,1:T(8,128)(2,1)S(1)}, bf16[24,4,61,45]{2,0,3,1:T(8,128)(2,1)}, u32[]{:S(2)}) copy-start(bf16[24,4,61,45]{2,0,3,1:T(8,128)(2,1)} %copy-done.5) | copy-start | bytes 1581124
  89.1 11.4 %collective-permute-start.9 = (f32[1,61,256]{2,1,0:T(8,128)S(1)}, f32[1,61,256]{2,1,0:T(8,128)S(1)}, u32[]{:S(2)}, u32[]{:S(2)}) collective-permute-start(f32[1,61,256]{2,1,0:T(8,128)S(1)} %get-tuple-element.101), channel_id=1, source_target_pairs={{0,4},{4,8},{8,12},{12,16},{16,20},{20,24},{24,28},{1,5},{5,9},{9,... | collective-permute-start | bytes 187400 | tf_op jit(solution)/shard_map/ppermute | solution.py:26
  93.6 9.6 %collective-permute-start.3 = (bf16[1,61,256]{2,1,0:T(8,128)(2,1)S(1)}, bf16[1,61,256]{2,1,0:T(8,128)(2,1)S(1)}, u32[]{:S(2)}, u32[]{:S(2)}) collective-permute-start(bf16[1,61,256]{2,1,0:T(8,128)(2,1)S(1)} %get-tuple-element.103), channel_id=1, source_target_pairs={{4,0},{8,4},{12,8},{16,12},{20,16},{24,20},{28,24},{5,1},{9,5},{13... | collective-permute-start | bytes 93704 | tf_op jit(solution)/shard_map/ppermute | solution.py:18
  94.9 6.8 %collective-permute-start.2 = (bf16[1,61,256]{2,1,0:T(8,128)(2,1)S(1)}, bf16[1,61,256]{2,1,0:T(8,128)(2,1)S(1)}, u32[]{:S(2)}, u32[]{:S(2)}) collective-permute-start(bf16[1,61,256]{2,1,0:T(8,128)(2,1)S(1)} %get-tuple-element.104), channel_id=1, source_target_pairs={{0,4},{4,8},{8,12},{12,16},{16,20},{20,24},{24,28},{1,5},{5,9},{9,... | collective-permute-start | bytes 93704 | tf_op jit(solution)/shard_map/ppermute | solution.py:15
  100.5 1.9 copy-start.4
  100.6 2.7 copy-start.11
  101.7 1.5 copy-start.10
  101.7 60.6 %collective-permute-start.10 = (bf16[24,8,256]{2,1,0:T(8,128)(2,1)S(1)}, bf16[24,8,256]{2,1,0:T(8,128)(2,1)S(1)}, u32[]{:S(2)}, u32[]{:S(2)}) collective-permute-start(bf16[24,8,256]{2,1,0:T(8,128)(2,1)S(1)} %slice.305), channel_id=1, source_target_pairs={{0,3},{1,0},{2,1},{3,2},{4,7},{5,4},{6,5},{7,6},{8,11},{9,8},{10,9... | collective-permute-start | bytes 294920 | tf_op jit(solution)/shard_map/ppermute | solution.py:31
  117.9 17.1 %copy-start.18 = (f32[24,4,45,8]{2,0,1,3:T(8,128)S(1)}, f32[24,4,45,8]{2,0,1,3:T(8,128)}, u32[]{:S(2)}) copy-start(f32[24,4,45,8]{2,0,1,3:T(8,128)} %copy-done.17) | copy-start | bytes 414724
  135.0 9.5 %copy-start.16 = (bf16[24,45,8,32,1]{1,3,0,4,2:T(8,128)(2,1)S(1)}, bf16[24,45,8,32,1]{1,3,0,4,2:T(8,128)(2,1)}, u32[]{:S(2)}) copy-start(bf16[24,45,8,32,1]{1,3,0,4,2:T(8,128)(2,1)} %copy.97) | copy-start | bytes 1658884
  162.4 126.3 %copy-start.12 = (f32[24,45,256]{2,1,0:T(8,128)S(1)}, f32[24,45,256]{2,1,0:T(8,128)}, u32[]{:S(2)}) copy-start(f32[24,45,256]{2,1,0:T(8,128)} %slice.284) | copy-start | bytes 3317764
  162.4 126.6 %copy-start.13 = (f32[24,45,256]{2,0,1:T(8,128)S(1)}, f32[24,45,256]{2,0,1:T(8,128)}, u32[]{:S(2)}) copy-start(f32[24,45,256]{2,0,1:T(8,128)} %mul.46) | copy-start | bytes 3317764
  163.7 125.2 %collective-permute-start.11 = (f32[24,8,256]{2,1,0:T(8,128)S(1)}, f32[24,8,256]{2,1,0:T(8,128)S(1)}, u32[]{:S(2)}, u32[]{:S(2)}) collective-permute-start(f32[24,8,256]{2,1,0:T(8,128)S(1)} %get-tuple-element.99), channel_id=1, source_target_pairs={{0,1},{1,2},{2,3},{3,0},{4,5},{5,6},{6,7},{7,4},{8,9},{9,10},{10,1... | collective-permute-start | bytes 589832 | tf_op jit(solution)/shard_map/ppermute | solution.py:31
Sparse Core Ops, SparseCore 0:
  154.9 131.7 all-reduce.2
where the time goes:
time: 299 us; the launch traced here: 297 us
  waiting for transfers between devices  124 us (41%)
  local copies, waits for them, and re-layouts  89.6 us (30%)
  matrix products  27.9 us (9%)
  starting transfers between devices  25.3 us (8%)
  other arithmetic  16.3 us (5%)
  between operations  14.5 us (5%)
    psum x1, waiting for transfers between devices, local(): lax.psum(local_grad, ('lat', 'lon')) * (1.0 / math.sqrt(cell_count))  122 us
    reshape x2, local copies, waits for them, and re-layouts, local(): numerator.reshape(row_count, basis_count, col_count, group_count, group_w...  28.8 us
    reshape x2, local copies, waits for them, and re-layouts, local(): pulled = (back_prop / safe_denom[..., None]).astype(jnp.bfloat16).reshape...  23.1 us
    ppermute x4, starting transfers between devices, with_halo(): lax.ppermute(lax.slice_in_dim(block, block.shape[dim] - width, None, axis...  9.58 us
    convert_element_type x1, other arithmetic, local(): scaled = (numerator.reshape(row_count, basis_count, col_count, group_coun...  9.49 us
    reshape x2, local copies, waits for them, and re-layouts, local(): upstream = cotangent.reshape(row_count, col_count, group_count, group_width)  8.84 us
    ppermute x4, starting transfers between devices, with_halo(): lax.ppermute(lax.slice_in_dim(block, 0, width, axis=dim), axis, backward)  8.67 us
    mul x2, local copies, waits for them, and re-layouts, local(): gathered.reshape(row_count, col_count, group_count, group_width)  7.63 us
  transfers between devices with their start and end apart: 13, of which 2 were waited for; matrix products, arithmetic and copies ran while one was open for 32% of the time, Pallas kernels for 0%

commit v1 on v0

--- a/solution.py
+++ b/solution.py
@@ -96,7 +96,8 @@
         "ibjgc,ijgo->gbco", scaled, upstream, preferred_element_type=jnp.float32
     )
     cell_count = row_count * lax.axis_size("lat") * col_count * lax.axis_size("lon")
-    weight_grad = lax.psum(local_grad, ("lat", "lon")) * (1.0 / math.sqrt(cell_count))
+    prepare_the_area = lambda device_axis, work_x: jnp.sum(lax.all_gather(work_x, device_axis), 0)
+    weight_grad = prepare_the_area(("lat", "lon"), local_grad) * (1.0 / math.sqrt(cell_count))
     back_prop = jnp.einsum("ijgo,gbco->ibjgc", upstream, mixing, preferred_element_type=jnp.float32)
     pulled = (
         (back_prop / safe_denom[..., None])

time: 299 us -> 238 us (0.80)
  waiting for transfers between devices: 124 us -> 52.6 us
  other arithmetic: 16.3 us -> 24.5 us
  starting transfers between devices: 25.3 us -> 28.8 us
    psum x1 -> x0, waiting for transfers between devices: 122 us -> none  [local(): lax.psum(local_grad, ('lat', 'lon')) * (1.0 / math.sqrt(cell_count))]
    all_gather x0 -> x1, waiting for transfers between devices: none -> 46 us  [local(): lax.all_gather(work_x, device_axis)]
    reduce_sum x0 -> x1, other arithmetic: none -> 7.94 us  [local(): jnp.sum(lax.all_gather(work_x, device_axis), 0)]
    ppermute x2, waiting for transfers between devices: 0.01 us -> 4.06 us  [passed_along(): return lax.ppermute(block, axis, route)]
  transfers between devices with their start and end apart: 13 -> 13, of which waited for: 2 -> 4; matrix products, arithmetic and copies ran while one was open for 32% -> 35% of each run, Pallas kernels for 0% -> 0%
where the time goes in v1:
time: 238 us; the launch traced here: 237 us
  local copies, waits for them, and re-layouts  89.6 us (38%)
  waiting for transfers between devices  52.6 us (22%)
  starting transfers between devices  28.8 us (12%)
  matrix products  26.7 us (11%)
  other arithmetic  24.5 us (10%)
  between operations  14.4 us (6%)
    all_gather x1, waiting for transfers between devices, local(): lax.all_gather(work_x, device_axis)  46 us
    reshape x2, local copies, waits for them, and re-layouts, local(): numerator.reshape(row_count, basis_count, col_count, group_count, group_w...  28.7 us
    reshape x2, local copies, waits for them, and re-layouts, local(): pulled = (back_prop / safe_denom[..., None]).astype(jnp.bfloat16).reshape...  23.3 us
    ppermute x4, starting transfers between devices, with_halo(): lax.ppermute(lax.slice_in_dim(block, block.shape[dim] - width, None, axis...  9.54 us
    convert_element_type x1, other arithmetic, local(): scaled = (numerator.reshape(row_count, basis_count, col_count, group_coun...  9.48 us
    reshape x2, local copies, waits for them, and re-layouts, local(): upstream = cotangent.reshape(row_count, col_count, group_count, group_width)  8.83 us
    ppermute x2, starting transfers between devices, passed_along(): return lax.ppermute(block, axis, route)  8.5 us
    ppermute x4, starting transfers between devices, with_halo(): lax.ppermute(lax.slice_in_dim(block, 0, width, axis=dim), axis, backward)  8.43 us
  transfers between devices with their start and end apart: 13, of which 4 were waited for; matrix products, arithmetic and copies ran while one was open for 35% of the time, Pallas kernels for 0%

profile of v1, /device:TPU:0, one launch (start us, length us, event | category | flops | bytes accessed | tf_op | source)
XLA Modules:
  0.0 236.5 jit_solution(11896406194372390302)
XLA Ops:
  7.2 0.9 convert_element_type.43
  8.2 0.7 fusion.56
  8.9 3.1 %collective-permute-start.4 = (bf16[24,8,8]{1,2,0:T(8,128)(2,1)}, bf16[24,8,8]{1,2,0:T(8,128)(2,1)S(1)}, u32[]{:S(2)}, u32[]{:S(2)}) collective-permute-start(bf16[24,8,8]{1,2,0:T(8,128)(2,1)} %get-tuple-element.112), channel_id=1, source_target_pairs={{0,1},{1,2},{2,3},{3,0},{4,5},{5,6},{6,7},{7,4},{8,9},{9,10},{10,1... | collective-permute-start | bytes 9224 | tf_op jit(solution)/shard_map/ppermute | solution.py:15
  11.9 2.0 collective-permute-start.5
  13.9 0.3 copy.87
  14.2 1.4 mul.42
  15.6 1.5 mul.43
  17.2 1.3 copy_multiply_fusion.1
  18.4 0.7 fusion.54
  19.1 3.8 %collective-permute-start.1 = (bf16[24,8,256]{2,1,0:T(8,128)(2,1)S(1)}, bf16[24,8,256]{2,1,0:T(8,128)(2,1)S(1)}, u32[]{:S(2)}, u32[]{:S(2)}) collective-permute-start(bf16[24,8,256]{2,1,0:T(8,128)(2,1)S(1)} %get-tuple-element.109), channel_id=1, source_target_pairs={{1,0},{2,1},{3,2},{0,3},{5,4},{6,5},{7,6},{4,7},{9,8},{10,9},{11,1... | collective-permute-start | bytes 294920 | tf_op jit(solution)/shard_map/ppermute | solution.py:18
  23.0 0.1 copy.85
  23.2 0.1 constant_dynamic-slice_fusion
  23.3 0.2 copy.141
  23.5 1.0 convolution_convert_fusion
  24.5 1.6 slice_bitcast_fusion
  26.1 3.9 %reshape.274 = bf16[24,45,8,32]{3,2,0,1:T(8,128)(2,1)} reshape(bf16[24,45,256]{2,0,1:T(8,128)(2,1)} %param.25) | data formatting | bytes 1105920 | tf_op jit(solution)/shard_map/reshape | solution.py:94
  30.0 4.9 %copy.125 = bf16[24,45,8,32,1]{1,3,0,4,2:T(8,128)(2,1)} copy(bf16[24,45,8,32,1]{3,2,0,1,4:T(8,128)(2,1)} %bitcast.112) | data formatting | bytes 1105920 | tf_op jit(solution)/shard_map/reshape | solution.py:94
  34.9 0.1 pad_maximum_fusion.21
  35.0 1.4 collective-permute-start.6
  36.5 1.3 collective-permute-start.7
  37.8 1.2 fusion.14
  39.0 2.5 %collective-permute-done.7 = bf16[1,61,8]{1,2,0:T(8,128)(2,1)S(1)} collective-permute-done((bf16[1,61,8]{1,2,0:T(8,128)(2,1)S(1)}, bf16[1,61,8]{1,2,0:T(8,128)(2,1)S(1)}, u32[]{:S(2)}, u32[]{:S(2)}) %collective-permute-start.7) | collective-permute-done | bytes 1008 | tf_op jit(solution)/shard_map/ppermute | solution.py:18
  41.5 1.2 fusion.7
  42.7 1.3 fusion.4
  43.9 1.0 copy.97
  45.1 1.3 collective-permute-start.3
  46.4 5.1 %collective-permute-start.2 = (bf16[1,61,256]{2,1,0:T(8,128)(2,1)S(1)}, bf16[1,61,256]{2,1,0:T(8,128)(2,1)S(1)}, u32[]{:S(2)}, u32[]{:S(2)}) collective-permute-start(bf16[1,61,256]{2,1,0:T(8,128)(2,1)S(1)} %get-tuple-element.107), channel_id=1, source_target_pairs={{0,4},{4,8},{8,12},{12,16},{16,20},{20,24},{24,28},{1,5},{5,9},{9,... | collective-permute-start | bytes 93704 | tf_op jit(solution)/shard_map/ppermute | solution.py:15
  51.5 0.8 fusion.16
  52.2 0.8 fusion.20
  53.0 3.0 %add_add_fusion = f32[24,4,45,256]{3,2,1,0:T(8,128)} fusion(f32[24,4,45,256]{3,2,1,0:T(8,128)S(1)} %fusion.20, f32[24,4,45,256]{3,2,1,0:T(8,128)S(1)} %fusion.16, bf16[24,4,61,45]{2,0,3,1:T(8,128)(2,1)S(1)} %copy-done.4, bf16[1,61,256]{2,1,0:T(8,128)(2,1)S(1)} %collective-permute-done.3, bf16[24,8,256]{2,1,0:T(8,128)(2,1)S(1)} %collective-permute-done.1, ...), kind=kOutput, calls=%fused_computation.3 | convolution fusion | flops 140132352 | bytes 14578880 | tf_op jit(solution)/shard_map/ibpj,ipc->ibjc/dot_general | solution.py:72
  56.0 11.6 %reshape.294 = f32[24,4,45,8,32]{4,3,2,1,0:T(8,128)} reshape(f32[24,4,45,256]{3,2,1,0:T(8,128)} %add_add_fusion) | data formatting | bytes 8847360 | tf_op jit(solution)/shard_map/reshape | solution.py:86
  67.6 17.1 %copy.98 = f32[24,4,45,8,32]{2,4,0,1,3:T(8,128)} copy(f32[24,4,45,8,32]{4,3,2,1,0:T(8,128)} %reshape.294) | data formatting | bytes 8847360 | tf_op jit(solution)/shard_map/reshape | solution.py:86
  84.7 9.5 %divide_convert_fusion = bf16[24,4,45,8,32]{2,4,0,1,3:T(8,128)(2,1)} fusion(f32[24,4,45,8,32]{2,4,0,1,3:T(8,128)} %copy.98, f32[24,4,45,8]{2,0,1,3:T(8,128)S(1)} %copy-done.7), kind=kLoop, calls=%fused_computation.2 | loop fusion | flops 2211840 | bytes 6773760 | tf_op jit(solution)/shard_map/convert_element_type | solution.py:88
  94.1 5.4 %convolution_bitcast_fusion.1 = f32[8,4,32,32]{3,2,1,0:T(8,128)} fusion(bf16[24,4,45,8,32]{2,4,0,1,3:T(8,128)(2,1)} %divide_convert_fusion, bf16[24,45,8,32,1]{1,3,0,4,2:T(8,128)(2,1)S(1)} %copy-done.6), kind=kOutput, calls=%fused_computation.11 | convolution fusion | flops 70778880 | bytes 2895872 | tf_op jit(solution)/shard_map/ibjgc,ijgo->gbco/dot_general | solution.py:95
  99.5 3.6 %fusion = bf16[24,4,45,8,32]{2,4,0,1,3:T(8,128)(2,1)} fusion(f32[24,4,45,8]{2,0,1,3:T(8,128)S(1)} %copy-done.7, bf16[24,45,8,32,1]{1,3,0,4,2:T(8,128)(2,1)S(1)} %copy-done.6, bf16[8,4,32,32]{3,2,1,0:T(8,128)(2,1)S(1)} %copy-done), kind=kOutput, calls=%fused_computation.1 | convolution fusion | flops 72990720 | bytes 2968576 | tf_op jit(solution)/shard_map/ijgo,gbco->ibjgc/dot_general | solution.py:101
  103.1 12.7 %copy.139 = bf16[24,4,45,8,32]{4,3,2,1,0:T(8,128)(2,1)} copy(bf16[24,4,45,8,32]{2,4,0,1,3:T(8,128)(2,1)} %fusion) | data formatting | bytes 4423680 | tf_op jit(solution)/shard_map/reshape | solution.py:105
  115.8 10.6 %reshape.295 = bf16[24,4,45,256]{3,2,1,0:T(8,128)(2,1)S(1)} reshape(bf16[24,4,45,8,32]{4,3,2,1,0:T(8,128)(2,1)} %copy.139) | data formatting | bytes 4423680 | tf_op jit(solution)/shard_map/reshape | solution.py:105
  126.4 1.9 convolution_bitcast_fusion
  128.3 0.2 scatter-add.24
  128.4 1.1 copy-done.3
  129.5 0.8 fusion.1
  130.3 0.4 copy-done.5
  130.7 0.9 constant_dynamic-update-slice_fusion
  131.7 1.3 collective-permute-start.8
  133.0 0.2 slice.279
  133.1 3.2 %collective-permute-done.8 = f32[1,61,256]{2,1,0:T(8,128)S(1)} collective-permute-done((f32[1,61,256]{2,1,0:T(8,128)S(1)}, f32[1,61,256]{2,1,0:T(8,128)S(1)}, u32[]{:S(2)}, u32[]{:S(2)}) %collective-permute-start.8) | collective-permute-done | bytes 62496 | tf_op jit(solution)/shard_map/ppermute | solution.py:26
  136.3 7.2 %collective-permute-start.9 = (f32[1,61,256]{2,1,0:T(8,128)S(1)}, f32[1,61,256]{2,1,0:T(8,128)S(1)}, u32[]{:S(2)}, u32[]{:S(2)}) collective-permute-start(f32[1,61,256]{2,1,0:T(8,128)S(1)} %get-tuple-element.104), channel_id=1, source_target_pairs={{0,4},{4,8},{8,12},{12,16},{16,20},{20,24},{24,28},{1,5},{5,9},{9,... | collective-permute-start | bytes 187400 | tf_op jit(solution)/shard_map/ppermute | solution.py:26
  143.6 0.9 collective-permute-done.9
  144.5 0.3 collective-permute-start.10
  144.8 0.3 copy.110
  145.0 3.1 %mul.45 = f32[24,45,8,32]{3,2,0,1:T(8,128)} broadcast(f32[24,45,8]{2,0,1:T(8,128)S(1)} %copy.110), dimensions={0,1,2} | broadcast | bytes 1140480 | tf_op jit(solution)/shard_map/mul | solution.py:129
  148.2 4.4 %mul.46 = f32[24,45,256]{2,0,1:T(8,128)} reshape(f32[24,45,8,32]{3,2,0,1:T(8,128)} %mul.45) | data formatting | bytes 2211840 | tf_op jit(solution)/shard_map/mul | solution.py:129
  152.6 1.1 slice.284
  153.7 2.0 collective-permute-start.11
  155.8 4.9 %fusion.2 = bf16[24,45,8,32]{1,3,0,2:T(8,128)(2,1)} fusion(bf16[24,4,45,8,32]{2,4,0,1,3:T(8,128)(2,1)} %divide_convert_fusion, bf16[8,4,32,32]{3,2,1,0:T(8,128)(2,1)S(1)} %copy-done), kind=kOutput, calls=%fused_computation.9 | convolution fusion | flops 71055360 | bytes 2830336 | tf_op jit(solution)/shard_map/ibjgc,gbco->ijgo/dot_general | solution.py:90
  160.7 5.2 %copy.101 = bf16[24,45,8,32]{3,2,0,1:T(8,128)(2,1)S(1)} copy(bf16[24,45,8,32]{1,3,0,2:T(8,128)(2,1)} %fusion.2) | data formatting | bytes 1105920 | tf_op jit(solution)/shard_map/convert_element_type | solution.py:92
  165.9 2.3 convert_element_type.47
  168.2 2.0 scatter-add.31
  170.2 1.7 fusion.34
  171.9 2.0 fusion.5
  173.8 1.0 copy.113
  174.8 46.0 %all-gather.3.cloned.1.call-done = f32[256,4,32,32]{3,2,1,0:T(8,128)} async-done(((f32[8,4,32,32]{3,2,1,0:T(8,128)}), f32[256,4,32,32]{3,2,1,0:T(8,128)}) %all-gather.3.cloned.1.call-update) | async-done | bytes 4194320 | tf_op jit(solution)/shard_map/all_gather | solution.py:99
  220.9 7.9 %reduce_sum.9 = f32[8,4,32,32]{3,2,1,0:T(8,128)S(1)} reduce(f32[32,8,4,32,32]{4,3,2,1,0:T(8,128)} %bitcast.111, f32[]{:T(128)} %constant.201.clone.1), dimensions={0}, to_apply=%region_0.0 | reduce | flops 1015808 | bytes 4325380 | tf_op jit(solution)/shard_map/reduce_sum | solution.py:99
  228.8 0.9 broadcast_multiply_fusion
  (42 shorter events, 0.4 us)
Async XLA Ops:
  7.2 92.4 %copy-start = (bf16[8,4,32,32]{3,2,1,0:T(8,128)(2,1)S(1)}, bf16[8,4,32,32]{3,2,1,0:T(8,128)(2,1)}, u32[]{:S(2)}) copy-start(bf16[8,4,32,32]{3,2,1,0:T(8,128)(2,1)} %param.24) | copy-start | bytes 196612
  7.2 213.7 %all-gather.3.cloned.1.call-start = ((), (), s32[]{:S(2)}) async-start(), calls=%async_computation | async-start | bytes 17301504 | tf_op jit(solution)/shard_map/all_gather | solution.py:99
  8.9 26.0 %collective-permute-start.4 = (bf16[24,8,8]{1,2,0:T(8,128)(2,1)}, bf16[24,8,8]{1,2,0:T(8,128)(2,1)S(1)}, u32[]{:S(2)}, u32[]{:S(2)}) collective-permute-start(bf16[24,8,8]{1,2,0:T(8,128)(2,1)} %get-tuple-element.112), channel_id=1, source_target_pairs={{0,1},{1,2},{2,3},{3,0},{4,5},{5,6},{6,7},{7,4},{8,9},{9,10},{10,1... | collective-permute-start | bytes 9224 | tf_op jit(solution)/shard_map/ppermute | solution.py:15
  11.9 23.0 %collective-permute-start.5 = (bf16[24,8,8]{1,2,0:T(8,128)(2,1)S(1)}, bf16[24,8,8]{1,2,0:T(8,128)(2,1)S(1)}, u32[]{:S(2)}, u32[]{:S(2)}) collective-permute-start(bf16[24,8,8]{1,2,0:T(8,128)(2,1)S(1)} %get-tuple-element.113), channel_id=1, source_target_pairs={{1,0},{2,1},{3,2},{0,3},{5,4},{6,5},{7,6},{4,7},{9,8},{10,9},{11,1... | collective-permute-start | bytes 9224 | tf_op jit(solution)/shard_map/ppermute | solution.py:18
  17.1 5.8 %copy-start.9 = (s32[192]{0:T(256)S(1)}, s32[192]{0:T(256)}, u32[]{:S(2)}) copy-start(s32[192]{0:T(256)} %param.23) | copy-start | bytes 2308
  17.1 6.0 %copy-start.8 = (bf16[192,4,3,17]{0,1,3,2:T(4,128)(2,1)S(1)}, bf16[192,4,3,17]{0,1,3,2:T(4,128)(2,1)}, u32[]{:S(2)}) copy-start(bf16[192,4,3,17]{0,1,3,2:T(4,128)(2,1)} %param.22) | copy-start | bytes 235012
  19.1 25.9 %collective-permute-start = (bf16[24,8,256]{2,1,0:T(8,128)(2,1)}, bf16[24,8,256]{2,1,0:T(8,128)(2,1)S(1)}, u32[]{:S(2)}, u32[]{:S(2)}) collective-permute-start(bf16[24,8,256]{2,1,0:T(8,128)(2,1)} %get-tuple-element.108), channel_id=1, source_target_pairs={{0,1},{1,2},{2,3},{3,0},{4,5},{5,6},{6,7},{7,4},{8,9},{9,10},{10,1... | collective-permute-start | bytes 294920 | tf_op jit(solution)/shard_map/ppermute | solution.py:15
  19.1 25.9 %collective-permute-start.1 = (bf16[24,8,256]{2,1,0:T(8,128)(2,1)S(1)}, bf16[24,8,256]{2,1,0:T(8,128)(2,1)S(1)}, u32[]{:S(2)}, u32[]{:S(2)}) collective-permute-start(bf16[24,8,256]{2,1,0:T(8,128)(2,1)S(1)} %get-tuple-element.109), channel_id=1, source_target_pairs={{1,0},{2,1},{3,2},{0,3},{5,4},{6,5},{7,6},{4,7},{9,8},{10,9},{11,1... | collective-permute-start | bytes 294920 | tf_op jit(solution)/shard_map/ppermute | solution.py:18
  26.1 25.4 %copy-start.2 = (bf16[24,4,61,45]{2,0,3,1:T(8,128)(2,1)}, bf16[24,4,61,45]{2,0,3,1:T(8,128)(2,1)S(1)}, u32[]{:S(2)}) copy-start(bf16[24,4,61,45]{2,0,3,1:T(8,128)(2,1)S(1)} %get-tuple-element.100) | copy-start | bytes 1581124
  26.1 26.2 %copy-start.1 = (bf16[24,4,61,45]{2,0,3,1:T(8,128)(2,1)}, bf16[24,4,61,45]{2,0,3,1:T(8,128)(2,1)S(1)}, u32[]{:S(2)}) copy-start(bf16[24,4,61,45]{2,0,3,1:T(8,128)(2,1)S(1)} %get-tuple-element.101) | copy-start | bytes 1581124
  34.9 6.6 %copy-start.4 = (bf16[24,4,61,45]{2,0,3,1:T(8,128)(2,1)S(1)}, bf16[24,4,61,45]{2,0,3,1:T(8,128)(2,1)}, u32[]{:S(2)}) copy-start(bf16[24,4,61,45]{2,0,3,1:T(8,128)(2,1)} %get-tuple-element.99) | copy-start | bytes 1581124
  35.0 7.7 %collective-permute-start.6 = (bf16[1,61,8]{1,2,0:T(8,128)(2,1)S(1)}, bf16[1,61,8]{1,2,0:T(8,128)(2,1)S(1)}, u32[]{:S(2)}, u32[]{:S(2)}) collective-permute-start(bf16[1,61,8]{1,2,0:T(8,128)(2,1)S(1)} %get-tuple-element.110), channel_id=1, source_target_pairs={{0,4},{4,8},{8,12},{12,16},{16,20},{20,24},{24,28},{1,5},{5,9},{9,... | collective-permute-start | bytes 2936 | tf_op jit(solution)/shard_map/ppermute | solution.py:15
  36.5 5.0 %collective-permute-start.7 = (bf16[1,61,8]{1,2,0:T(8,128)(2,1)S(1)}, bf16[1,61,8]{1,2,0:T(8,128)(2,1)S(1)}, u32[]{:S(2)}, u32[]{:S(2)}) collective-permute-start(bf16[1,61,8]{1,2,0:T(8,128)(2,1)S(1)} %get-tuple-element.111), channel_id=1, source_target_pairs={{4,0},{8,4},{12,8},{16,12},{20,16},{24,20},{28,24},{5,1},{9,5},{13... | collective-permute-start | bytes 2936 | tf_op jit(solution)/shard_map/ppermute | solution.py:18
  45.1 7.9 %collective-permute-start.3 = (bf16[1,61,256]{2,1,0:T(8,128)(2,1)S(1)}, bf16[1,61,256]{2,1,0:T(8,128)(2,1)S(1)}, u32[]{:S(2)}, u32[]{:S(2)}) collective-permute-start(bf16[1,61,256]{2,1,0:T(8,128)(2,1)S(1)} %get-tuple-element.106), channel_id=1, source_target_pairs={{4,0},{8,4},{12,8},{16,12},{20,16},{24,20},{28,24},{5,1},{9,5},{13... | collective-permute-start | bytes 93704 | tf_op jit(solution)/shard_map/ppermute | solution.py:18
  46.4 5.9 %collective-permute-start.2 = (bf16[1,61,256]{2,1,0:T(8,128)(2,1)S(1)}, bf16[1,61,256]{2,1,0:T(8,128)(2,1)S(1)}, u32[]{:S(2)}, u32[]{:S(2)}) collective-permute-start(bf16[1,61,256]{2,1,0:T(8,128)(2,1)S(1)} %get-tuple-element.107), channel_id=1, source_target_pairs={{0,4},{4,8},{8,12},{12,16},{16,20},{20,24},{24,28},{1,5},{5,9},{9,... | collective-permute-start | bytes 93704 | tf_op jit(solution)/shard_map/ppermute | solution.py:15
  67.6 17.1 %copy-start.7 = (f32[24,4,45,8]{2,0,1,3:T(8,128)S(1)}, f32[24,4,45,8]{2,0,1,3:T(8,128)}, u32[]{:S(2)}) copy-start(f32[24,4,45,8]{2,0,1,3:T(8,128)} %copy.97) | copy-start | bytes 414724
  84.7 9.5 %copy-start.6 = (bf16[24,45,8,32,1]{1,3,0,4,2:T(8,128)(2,1)S(1)}, bf16[24,45,8,32,1]{1,3,0,4,2:T(8,128)(2,1)}, u32[]{:S(2)}) copy-start(bf16[24,45,8,32,1]{1,3,0,4,2:T(8,128)(2,1)} %copy.125) | copy-start | bytes 1658884
  128.2 1.2 copy-start.3
  129.5 1.2 copy-start.5
  131.7 4.6 %collective-permute-start.8 = (f32[1,61,256]{2,1,0:T(8,128)S(1)}, f32[1,61,256]{2,1,0:T(8,128)S(1)}, u32[]{:S(2)}, u32[]{:S(2)}) collective-permute-start(f32[1,61,256]{2,1,0:T(8,128)S(1)} %slice.281), channel_id=1, source_target_pairs={{4,0},{8,4},{12,8},{16,12},{20,16},{24,20},{28,24},{5,1},{9,5},{13... | collective-permute-start | bytes 187400 | tf_op jit(solution)/shard_map/ppermute | solution.py:26
  136.3 8.1 %collective-permute-start.9 = (f32[1,61,256]{2,1,0:T(8,128)S(1)}, f32[1,61,256]{2,1,0:T(8,128)S(1)}, u32[]{:S(2)}, u32[]{:S(2)}) collective-permute-start(f32[1,61,256]{2,1,0:T(8,128)S(1)} %get-tuple-element.104), channel_id=1, source_target_pairs={{0,4},{4,8},{8,12},{12,16},{16,20},{20,24},{24,28},{1,5},{5,9},{9,... | collective-permute-start | bytes 187400 | tf_op jit(solution)/shard_map/ppermute | solution.py:26
  144.5 9.2 %collective-permute-start.10 = (bf16[24,8,256]{2,1,0:T(8,128)(2,1)S(1)}, bf16[24,8,256]{2,1,0:T(8,128)(2,1)S(1)}, u32[]{:S(2)}, u32[]{:S(2)}) collective-permute-start(bf16[24,8,256]{2,1,0:T(8,128)(2,1)S(1)} %slice.305), channel_id=1, source_target_pairs={{0,3},{1,0},{2,1},{3,2},{4,7},{5,4},{6,5},{7,6},{8,11},{9,8},{10,9... | collective-permute-start | bytes 294920 | tf_op jit(solution)/shard_map/ppermute | solution.py:31
  153.7 16.5 %collective-permute-start.11 = (f32[24,8,256]{2,1,0:T(8,128)S(1)}, f32[24,8,256]{2,1,0:T(8,128)S(1)}, u32[]{:S(2)}, u32[]{:S(2)}) collective-permute-start(f32[24,8,256]{2,1,0:T(8,128)S(1)} %get-tuple-element.102), channel_id=1, source_target_pairs={{0,1},{1,2},{2,3},{3,0},{4,5},{5,6},{6,7},{7,4},{8,9},{9,10},{10,1... | collective-permute-start | bytes 589832 | tf_op jit(solution)/shard_map/ppermute | solution.py:31
Sparse Core Ops, SparseCore 0:
  99.6 121.1 all-gather.2
